TPU v7x, 32 devices: a whole 2x2x4 slice. The times are simulated.
32 devices in a mesh: tm: 8 (over z, y), col: 4 (over x, core).
Axes of the slice: x: 2, y: 2, z: 4, core: 2. Of those that a mesh axis runs over, the one named last changes fastest.
Arguments:
- observed: bfloat16 [16, 128, 512], P('tm', None, 'col'), may hold values from -6 to 6
- input_gain: float32 [512], P('col'), may hold values from 0.03 to 0.3
- persist: float32 [16, 512], P('tm', 'col'), may hold values from 0.5 to 1, as said below
- coupling: bfloat16 [16, 512, 512], P('tm', None, 'col'), may hold values from -0.02734375 to 0.02734375
- pattern: int32 [8, 8], replicated, may hold values 0 or 1
Outputs:
- filtered: float32 [16, 128, 512], P('tm', None, 'col')
- smoothed: float32 [16, 128, 512], P('tm', None, 'col')
Inputs may be any that keep to these rules, and one draw needn't show every extreme that they name: `persist`: persistence of each state component at each step.
All inputs are finite; a program needn't handle non-finite values.
Results may differ from a plain program's by a relative error of at most 0.0003.
Values may be sent and summed in bfloat16 or wider, within the bound.
No kernel may reach another device: no remote copies, remote signals or barrier semaphores. Data moves between devices by JAX's collectives and lax.ppermute only.
A program may use at most 64 MiB of HBM per device.

v0:
```python
import jax
import jax.numpy as jnp
from jax import lax
from jax.sharding import PartitionSpec as P


def passed_along(shard, axis, by):
    length = lax.axis_size(axis)
    pairs = [(i, i + by) for i in range(length) if 0 <= i + by < length]
    return lax.ppermute(shard, axis, pairs)


def matmul(left, right):
    return jnp.dot(left, right, precision=lax.Precision.HIGHEST, preferred_element_type=jnp.float32)


def advance(state, matrix):
    return matmul(lax.all_gather(state, "col", axis=1, tiled=True), matrix)


def smooth_step(later, state_full, state_part, cols_matrix, rows_matrix):
    predicted = matmul(state_full, cols_matrix)
    residual = later - predicted
    residual_full = lax.all_gather(residual, "col", axis=1, tiled=True)
    return state_part + matmul(residual_full, rows_matrix.T)


def local(observed, input_gain, persist, coupling, pattern):
    step_count = observed.shape[0]
    panels = observed.shape[1]
    state_width = coupling.shape[1]
    col_count = coupling.shape[2]
    block_count = pattern.shape[0]
    block_size = state_width // block_count
    col_pos = lax.axis_index("col")
    tm_pos = lax.axis_index("tm")
    time_block_groups = lax.axis_size("tm")
    first_col = col_pos * col_count
    pattern_real = pattern.astype(jnp.float32)
    row_ids = jnp.arange(state_width)
    col_ids = first_col + jnp.arange(col_count)
    block_labels = jnp.arange(block_count)
    row_hot = (row_ids[:, None] // block_size == block_labels[None, :]).astype(jnp.float32)
    col_hot = (col_ids[:, None] // block_size == block_labels[None, :]).astype(jnp.float32)
    mask_cols = matmul(matmul(row_hot, pattern_real), col_hot.T)
    mask_rows = matmul(matmul(col_hot, pattern_real), row_hot.T)
    diag_cols = (row_ids[:, None] == col_ids[None, :]).astype(jnp.float32)
    diag_rows = diag_cols.T
    trans_cols = (
        coupling.astype(jnp.float32) * mask_cols[None] + diag_cols[None] * persist[:, None, :]
    )
    rows_coupling = lax.all_to_all(coupling, "col", split_axis=1, concat_axis=2, tiled=True)
    trans_rows = (
        rows_coupling.astype(jnp.float32) * mask_rows[None] + diag_rows[None] * persist[:, :, None]
    )
    driven = input_gain[None, None, :] * observed.astype(jnp.float32)
    top_zeros = jnp.zeros((state_width, col_count), jnp.float32)
    state = jnp.concatenate([diag_cols, jnp.zeros((panels, col_count), jnp.float32)], axis=0)
    history = []
    for position in range(step_count):
        state = advance(state, trans_cols[position]) + jnp.concatenate(
            [top_zeros, driven[position]], axis=0
        )
        history.append(state)
    stacked_rows = jnp.stack(history)
    element = history[-1]
    saved = []
    stride = 1
    whole = lax.all_gather(element, "col", axis=1, tiled=True)
    whole_zeros = jnp.zeros((state_width, state_width), jnp.float32)
    while stride < time_block_groups:
        own_prod = whole[:state_width]
        saved.append(lax.dynamic_slice_in_dim(own_prod, first_col, col_count, 1))
        prior_values = passed_along(whole, "tm", stride)
        joined = matmul(prior_values, own_prod) + jnp.concatenate(
            [whole_zeros, whole[state_width:]], axis=0
        )
        whole = jnp.where(tm_pos >= stride, joined, whole)
        stride = stride * 2
    end_slice = lax.dynamic_slice_in_dim(whole[state_width:], first_col, col_count, 1)
    start_slice = passed_along(end_slice, "tm", 1)
    start_full = lax.all_gather(start_slice, "col", axis=1, tiled=True)
    filtered = (
        jnp.einsum(
            "bs,lsc->lbc",
            start_full,
            stacked_rows[:, :state_width],
            precision=lax.Precision.HIGHEST,
        )
        + stacked_rows[:, state_width:]
    )
    filtered_full = lax.all_gather(filtered, "col", axis=2, tiled=True)
    later = jnp.zeros((panels, col_count), jnp.float32)
    for position in range(step_count - 1, -1, -1):
        if position > 0:
            later = smooth_step(
                later,
                filtered_full[position - 1],
                filtered[position - 1],
                trans_cols[position],
                trans_rows[position],
            )
        else:
            later = smooth_step(
                later, start_full, start_slice, trans_cols[position], trans_rows[position]
            )
    offset = later
    from_next = passed_along(offset, "tm", -1)
    carried = jnp.where(tm_pos == time_block_groups - 1, filtered[step_count - 1], from_next)
    stride = 1
    for level_prod in saved:
        partial_value = matmul(carried, level_prod.T)
        shares = lax.psum_scatter(partial_value, "col", scatter_dimension=1, tiled=True)
        carried = carried + passed_along(shares, "tm", -stride)
        stride = stride * 2
    later = carried
    smoothed_list = [carried]
    position = 1
    later = smooth_step(
        later,
        filtered_full[position - 1],
        filtered[position - 1],
        trans_cols[position],
        trans_rows[position],
    )
    smoothed_list.append(later)
    smoothed = jnp.stack(smoothed_list[::-1])
    return (filtered, smoothed)


def solution(mesh):
    return jax.shard_map(
        local,
        mesh=mesh,
        in_specs=(P("tm", None, "col"), P("col"), P("tm", "col"), P("tm", None, "col"), P()),
        out_specs=(P("tm", None, "col"), P("tm", None, "col")),
        check_vma=False,
    )
```

profile of v0, /device:TPU:0, one launch (start us, length us, event | category | flops | bytes accessed | tf_op | source)
XLA Modules:
  0.0 347.9 jit_solution(4081061395193366817)
XLA Ops:
  10.4 20.2 %all-gather.4.cloned.1.call-done = f32[640,512]{1,0:T(8,128)} async-done(((f32[640,128]{1,0:T(8,128)}), f32[640,512]{1,0:T(8,128)}) %all-gather.4.cloned.1.call-update) | async-done | bytes 1310736 | tf_op jit(solution)/shard_map/all_gather | solution.py:18
  33.9 18.4 %all-gather.6.cloned.1.call-done = f32[640,512]{1,0:T(8,128)} async-done(((f32[640,128]{1,0:T(8,128)}), f32[640,512]{1,0:T(8,128)}) %all-gather.6.cloned.1.call-update) | async-done | bytes 1310736 | tf_op jit(solution)/shard_map/all_gather | solution.py:18
  55.6 18.5 %all-gather.8.cloned.1.call-done = f32[640,512]{1,0:T(8,128)} async-done(((f32[640,128]{1,0:T(8,128)}), f32[640,512]{1,0:T(8,128)}) %all-gather.8.cloned.1.call-update) | async-done | bytes 1310736 | tf_op jit(solution)/shard_map/all_gather | solution.py:69
  78.5 27.7 %collective-permute-done = f32[640,512]{1,0:T(8,128)S(1)} collective-permute-done((f32[640,512]{1,0:T(8,128)}, f32[640,512]{1,0:T(8,128)S(1)}, u32[]{:S(2)}, u32[]{:S(2)}) %collective-permute-start) | collective-permute-done | bytes 1310752 | tf_op jit(solution)/shard_map/ppermute | solution.py:10
  106.2 3.9 %fusion = f32[640,512]{1,0:T(8,128)S(1)} fusion(f32[640,512]{1,0:T(8,128)} %all-gather.8.cloned.1.call-done, f32[640,512]{1,0:T(8,128)S(1)} %collective-permute-done, f32[128,512]{1,0:T(8,128)S(1)} %slice.85, pred[]{:T(512)S(6)} %ge.11), kind=kOutput, calls=%fused_computation.2 | convolution fusion | flops 2013921280 | bytes 5242881 | tf_op jit(solution)/shard_map/dot_general | solution.py:14
  110.1 6.3 %collective-permute-start.1 = (f32[640,512]{1,0:T(8,128)S(1)}, f32[640,512]{1,0:T(8,128)}, u32[]{:S(2)}, u32[]{:S(2)}) collective-permute-start(f32[640,512]{1,0:T(8,128)S(1)} %fusion), channel_id=1, source_target_pairs={{0,8},{4,12},{8,16},{12,20},{16,24},{20,28},{1,9},{5,13},{9,17},{1... | collective-permute-start | bytes 3932168 | tf_op jit(solution)/shard_map/ppermute | solution.py:10
  116.5 26.5 %collective-permute-done.1 = f32[640,512]{1,0:T(8,128)} collective-permute-done((f32[640,512]{1,0:T(8,128)S(1)}, f32[640,512]{1,0:T(8,128)}, u32[]{:S(2)}, u32[]{:S(2)}) %collective-permute-start.1) | collective-permute-done | bytes 1310752 | tf_op jit(solution)/shard_map/ppermute | solution.py:10
  142.9 3.6 %fusion.1 = f32[640,512]{1,0:T(8,128)S(1)} fusion(f32[640,512]{1,0:T(8,128)S(1)} %fusion, f32[640,512]{1,0:T(8,128)} %collective-permute-done.1, f32[128,512]{1,0:T(8,128)S(1)} %slice.87, pred[]{:T(512)S(6)} %ge.10), kind=kOutput, calls=%fused_computation.3 | convolution fusion | flops 2013921280 | bytes 5242881 | tf_op jit(solution)/shard_map/dot_general | solution.py:14
  146.5 6.5 %collective-permute-start.2 = (f32[640,512]{1,0:T(8,128)S(1)}, f32[640,512]{1,0:T(8,128)}, u32[]{:S(2)}, u32[]{:S(2)}) collective-permute-start(f32[640,512]{1,0:T(8,128)S(1)} %fusion.1), channel_id=1, source_target_pairs={{0,16},{4,20},{8,24},{12,28},{1,17},{5,21},{9,25},{13,29},{2,18},{... | collective-permute-start | bytes 3932168 | tf_op jit(solution)/shard_map/ppermute | solution.py:10
  159.5 3.9 %all-to-all-done = bf16[2,512,128]{2,0,1:T(2,128)(2,1)S(1)} async-done(((bf16[2,512,128]{2,0,1:T(2,128)(2,1)}), bf16[2,512,128]{2,0,1:T(2,128)(2,1)S(1)}, u32[]{:S(2)}, u32[]{:S(2)}) %all-to-all-start) | async-done | bytes 262176 | tf_op jit(solution)/shard_map/all_to_all | solution.py:52
  166.3 12.4 %collective-permute-done.2 = f32[640,512]{1,0:T(8,128)} collective-permute-done((f32[640,512]{1,0:T(8,128)S(1)}, f32[640,512]{1,0:T(8,128)}, u32[]{:S(2)}, u32[]{:S(2)}) %collective-permute-start.2) | collective-permute-done | bytes 1310752 | tf_op jit(solution)/shard_map/ppermute | solution.py:10
  178.7 3.6 %fusion.39 = f32[640,512]{1,0:T(8,128)S(1)} fusion(f32[640,512]{1,0:T(8,128)} %collective-permute-done.2, f32[640,512]{1,0:T(8,128)S(1)} %fusion.1), kind=kOutput, calls=%fused_computation.80 | convolution fusion | flops 2013265920 | bytes 3670016 | tf_op jit(solution)/shard_map/dot_general | solution.py:14
  186.9 5.9 %all_gather.27 = f32[128,512]{1,0:T(8,128)S(1)} all-gather(f32[128,128]{1,0:T(8,128)S(1)} %collective-permute-done.3), channel_id=1, replica_groups=mesh['tm'=8,'col'=4] {'col'}, dimensions={1}, use_global_device_ids=true | all-gather | bytes 327680 | tf_op jit(solution)/shard_map/all_gather | solution.py:82
  193.3 7.3 %all_gather.28 = f32[2,128,512]{2,1,0:T(8,128)S(1)} all-gather(f32[2,128,128]{2,1,0:T(8,128)S(1)} %fusion.2), channel_id=1, replica_groups=mesh['tm'=8,'col'=4] {'col'}, dimensions={2}, use_global_device_ids=true | all-gather | bytes 655360 | tf_op jit(solution)/shard_map/all_gather | solution.py:92
  200.9 5.9 %all_gather.29 = f32[128,512]{1,0:T(8,128)S(1)} all-gather(f32[128,128]{1,0:T(8,128)S(1)} %get-tuple-element.6), channel_id=1, replica_groups=mesh['tm'=8,'col'=4] {'col'}, dimensions={1}, use_global_device_ids=true | all-gather | bytes 327680 | tf_op jit(solution)/shard_map/all_gather | solution.py:24
  207.6 5.9 %all_gather.30 = f32[128,512]{1,0:T(8,128)S(1)} all-gather(f32[128,128]{1,0:T(8,128)S(1)} %convolution_subtract_fusion), channel_id=1, replica_groups=mesh['tm'=8,'col'=4] {'col'}, dimensions={1}, use_global_device_ids=true | all-gather | bytes 327680 | tf_op jit(solution)/shard_map/all_gather | solution.py:24
  216.4 32.3 %collective-permute-done.4 = f32[128,128]{1,0:T(8,128)S(1)} collective-permute-done((f32[128,128]{1,0:T(8,128)S(1)}, f32[128,128]{1,0:T(8,128)S(1)}, u32[]{:S(2)}, u32[]{:S(2)}) %collective-permute-start.4) | collective-permute-done | bytes 65568 | tf_op jit(solution)/shard_map/ppermute | solution.py:10
  249.9 22.4 %reduce-scatter.4.cloned.1.call-done = f32[128,128]{1,0:T(8,128)} async-done(((f32[128,512]{1,0:T(8,128)}), f32[128,128]{1,0:T(8,128)}) %reduce-scatter.4.cloned.1.call-update) | async-done | bytes 65552 | tf_op jit(solution)/shard_map/reduce_scatter | solution.py:113
  273.6 5.0 %collective-permute-done.5 = f32[128,128]{1,0:T(8,128)S(1)} collective-permute-done((f32[128,128]{1,0:T(8,128)}, f32[128,128]{1,0:T(8,128)S(1)}, u32[]{:S(2)}, u32[]{:S(2)}) %collective-permute-start.5) | collective-permute-done | bytes 65568 | tf_op jit(solution)/shard_map/ppermute | solution.py:10
  279.8 20.2 %reduce-scatter.6.cloned.1.call-done = f32[128,128]{1,0:T(8,128)} async-done(((f32[128,512]{1,0:T(8,128)}), f32[128,128]{1,0:T(8,128)}) %reduce-scatter.6.cloned.1.call-update) | async-done | bytes 65552 | tf_op jit(solution)/shard_map/reduce_scatter | solution.py:113
  301.3 5.0 %collective-permute-done.6 = f32[128,128]{1,0:T(8,128)S(1)} collective-permute-done((f32[128,128]{1,0:T(8,128)}, f32[128,128]{1,0:T(8,128)S(1)}, u32[]{:S(2)}, u32[]{:S(2)}) %collective-permute-start.6) | collective-permute-done | bytes 65568 | tf_op jit(solution)/shard_map/ppermute | solution.py:10
  307.4 19.3 %reduce-scatter.8.cloned.1.call-done = f32[128,128]{1,0:T(8,128)} async-done(((f32[128,512]{1,0:T(8,128)}), f32[128,128]{1,0:T(8,128)}) %reduce-scatter.8.cloned.1.call-update) | async-done | bytes 65552 | tf_op jit(solution)/shard_map/reduce_scatter | solution.py:113
  328.0 6.3 %collective-permute-done.7 = f32[128,128]{1,0:T(8,128)S(1)} collective-permute-done((f32[128,128]{1,0:T(8,128)}, f32[128,128]{1,0:T(8,128)S(1)}, u32[]{:S(2)}, u32[]{:S(2)}) %collective-permute-start.7) | collective-permute-done | bytes 65568 | tf_op jit(solution)/shard_map/ppermute | solution.py:10
  334.3 5.8 %all_gather.31 = f32[128,512]{1,0:T(8,128)S(1)} all-gather(f32[128,128]{1,0:T(8,128)S(1)} %get-tuple-element.2), channel_id=1, replica_groups=mesh['tm'=8,'col'=4] {'col'}, dimensions={1}, use_global_device_ids=true | all-gather | bytes 327680 | tf_op jit(solution)/shard_map/all_gather | solution.py:24
  (84 shorter events, 41.0 us)
Async XLA Ops:
  7.2 3.1 copy-start.10
  7.2 23.4 %all-gather.4.cloned.1.call-start = ((), (), s32[]{:S(2)}) async-start(), calls=%async_computation.4 | async-start | bytes 1638400 | tf_op jit(solution)/shard_map/all_gather | solution.py:18
  8.1 44.3 %all-gather.6.cloned.1.call-start = ((), (), s32[]{:S(2)}) async-start(), calls=%async_computation.5 | async-start | bytes 1638400 | tf_op jit(solution)/shard_map/all_gather | solution.py:18
  33.9 40.2 %all-gather.8.cloned.1.call-start = ((), (), s32[]{:S(2)}) async-start(), calls=%async_computation.6 | async-start | bytes 1638400 | tf_op jit(solution)/shard_map/all_gather | solution.py:69
  74.1 32.1 %collective-permute-start = (f32[640,512]{1,0:T(8,128)}, f32[640,512]{1,0:T(8,128)S(1)}, u32[]{:S(2)}, u32[]{:S(2)}) collective-permute-start(f32[640,512]{1,0:T(8,128)} %all-gather.8.cloned.1.call-done), channel_id=1, source_target_pairs={{0,4},{4,8},{8,12},{12,16},{16,20},{20,24},{24,28},{1,5},{5,9},{9,... | collective-permute-start | bytes 3932168 | tf_op jit(solution)/shard_map/ppermute | solution.py:10
  110.1 32.8 %collective-permute-start.1 = (f32[640,512]{1,0:T(8,128)S(1)}, f32[640,512]{1,0:T(8,128)}, u32[]{:S(2)}, u32[]{:S(2)}) collective-permute-start(f32[640,512]{1,0:T(8,128)S(1)} %fusion), channel_id=1, source_target_pairs={{0,8},{4,12},{8,16},{12,20},{16,24},{20,28},{1,9},{5,13},{9,17},{1... | collective-permute-start | bytes 3932168 | tf_op jit(solution)/shard_map/ppermute | solution.py:10
  116.4 41.0 %copy-start.11 = (s32[8,8]{1,0:T(8,128)S(1)}, s32[8,8]{1,0:T(8,128)}, u32[]{:S(2)}) copy-start(s32[8,8]{1,0:T(8,128)} %param.9) | copy-start | bytes 772
  146.5 32.2 %collective-permute-start.2 = (f32[640,512]{1,0:T(8,128)S(1)}, f32[640,512]{1,0:T(8,128)}, u32[]{:S(2)}, u32[]{:S(2)}) collective-permute-start(f32[640,512]{1,0:T(8,128)S(1)} %fusion.1), channel_id=1, source_target_pairs={{0,16},{4,20},{8,24},{12,28},{1,17},{5,21},{9,25},{13,29},{2,18},{... | collective-permute-start | bytes 3932168 | tf_op jit(solution)/shard_map/ppermute | solution.py:10
  154.0 9.4 %all-to-all-start = ((bf16[2,512,128]{2,0,1:T(2,128)(2,1)}), bf16[2,512,128]{2,0,1:T(2,128)(2,1)S(1)}, u32[]{:S(2)}, u32[]{:S(2)}) async-start(bf16[2,512,128]{2,0,1:T(2,128)(2,1)} %copy.18), calls=%async_computation | async-start | bytes 524288 | tf_op jit(solution)/shard_map/all_to_all | solution.py:52
  157.4 114.9 %reduce-scatter.4.cloned.1.call-start = ((), (), s32[]{:S(2)}) async-start(), calls=%async_computation.7 | async-start | bytes 327680 | tf_op jit(solution)/shard_map/reduce_scatter | solution.py:113
  166.3 18.7 %copy-start.7 = (f32[128,512]{0,1:T(8,128)S(1)}, f32[128,512]{0,1:T(8,128)}, u32[]{:S(2)}) copy-start(f32[128,512]{0,1:T(8,128)} %fusion.15) | copy-start | bytes 786436
  166.3 18.7 %copy-start.8 = (f32[128,512]{0,1:T(8,128)S(1)}, f32[128,512]{0,1:T(8,128)}, u32[]{:S(2)}) copy-start(f32[128,512]{0,1:T(8,128)} %fusion.18) | copy-start | bytes 786436
  182.3 10.5 %copy-start = (f32[640,128]{1,0:T(8,128)S(1)}, f32[640,128]{1,0:T(8,128)}, u32[]{:S(2)}) copy-start(f32[640,128]{1,0:T(8,128)} %convolution_add_fusion.3) | copy-start | bytes 983044
  182.3 10.5 %copy-start.1 = (f32[640,128]{1,0:T(8,128)S(1)}, f32[640,128]{1,0:T(8,128)}, u32[]{:S(2)}) copy-start(f32[640,128]{1,0:T(8,128)} %convolution_add_fusion.2) | copy-start | bytes 983044
  182.3 4.5 %collective-permute-start.3 = (f32[128,128]{1,0:T(8,128)S(1)}, f32[128,128]{1,0:T(8,128)S(1)}, u32[]{:S(2)}, u32[]{:S(2)}) collective-permute-start(f32[128,128]{1,0:T(8,128)S(1)} %fusion.22), channel_id=1, source_target_pairs={{0,4},{4,8},{8,12},{12,16},{16,20},{20,24},{24,28},{1,5},{5,9},{9,... | collective-permute-start | bytes 196616 | tf_op jit(solution)/shard_map/ppermute | solution.py:10
  185.1 28.4 %copy-start.2 = (f32[2,128,512]{1,2,0:T(8,128)}, f32[2,128,512]{1,2,0:T(8,128)S(1)}, u32[]{:S(2)}) copy-start(f32[2,128,512]{1,2,0:T(8,128)S(1)} %fusion.6) | copy-start | bytes 1572868
  193.2 146.8 %copy-start.4 = (f32[2,128,128]{2,1,0:T(8,128)}, f32[2,128,128]{2,1,0:T(8,128)S(1)}, u32[]{:S(2)}) copy-start(f32[2,128,128]{2,1,0:T(8,128)S(1)} %fusion.2) | copy-start | bytes 393220
  213.8 34.9 %collective-permute-start.4 = (f32[128,128]{1,0:T(8,128)S(1)}, f32[128,128]{1,0:T(8,128)S(1)}, u32[]{:S(2)}, u32[]{:S(2)}) collective-permute-start(f32[128,128]{1,0:T(8,128)S(1)} %convolution_add_fusion.5), channel_id=1, source_target_pairs={{4,0},{8,4},{12,8},{16,12},{20,16},{24,20},{28,24},{5,1},{9,5},{13... | collective-permute-start | bytes 196616 | tf_op jit(solution)/shard_map/ppermute | solution.py:10
  249.8 50.1 %reduce-scatter.6.cloned.1.call-start = ((), (), s32[]{:S(2)}) async-start(), calls=%async_computation.8 | async-start | bytes 327680 | tf_op jit(solution)/shard_map/reduce_scatter | solution.py:113
  272.2 6.4 %collective-permute-start.5 = (f32[128,128]{1,0:T(8,128)}, f32[128,128]{1,0:T(8,128)S(1)}, u32[]{:S(2)}, u32[]{:S(2)}) collective-permute-start(f32[128,128]{1,0:T(8,128)} %reduce-scatter.4.cloned.1.call-done), channel_id=1, source_target_pairs={{4,0},{8,4},{12,8},{16,12},{20,16},{24,20},{28,24},{5,1},{9,5},{13... | collective-permute-start | bytes 196616 | tf_op jit(solution)/shard_map/ppermute | solution.py:10
  279.7 47.0 %reduce-scatter.8.cloned.1.call-start = ((), (), s32[]{:S(2)}) async-start(), calls=%async_computation.9 | async-start | bytes 327680 | tf_op jit(solution)/shard_map/reduce_scatter | solution.py:113
  299.9 6.4 %collective-permute-start.6 = (f32[128,128]{1,0:T(8,128)}, f32[128,128]{1,0:T(8,128)S(1)}, u32[]{:S(2)}, u32[]{:S(2)}) collective-permute-start(f32[128,128]{1,0:T(8,128)} %reduce-scatter.6.cloned.1.call-done), channel_id=1, source_target_pairs={{8,0},{12,4},{16,8},{20,12},{24,16},{28,20},{9,1},{13,5},{17,9},{2... | collective-permute-start | bytes 196616 | tf_op jit(solution)/shard_map/ppermute | solution.py:10
  301.3 38.7 %copy-start.3 = (f32[2,128,512]{1,2,0:T(8,128)S(1)}, f32[2,128,512]{1,2,0:T(8,128)}, u32[]{:S(2)}) copy-start(f32[2,128,512]{1,2,0:T(8,128)} %copy-done.2) | copy-start | bytes 1572868
  326.7 7.6 %collective-permute-start.7 = (f32[128,128]{1,0:T(8,128)}, f32[128,128]{1,0:T(8,128)S(1)}, u32[]{:S(2)}, u32[]{:S(2)}) collective-permute-start(f32[128,128]{1,0:T(8,128)} %reduce-scatter.8.cloned.1.call-done), channel_id=1, source_target_pairs={{16,0},{20,4},{24,8},{28,12},{17,1},{21,5},{25,9},{29,13},{18,2},{... | collective-permute-start | bytes 196616 | tf_op jit(solution)/shard_map/ppermute | solution.py:10
  (3 other events, 7.8 us)
Sparse Core Ops, SparseCore 0:
  9.6 21.0 all-gather.3
  34.0 18.3 all-gather.5
  55.7 18.3 all-gather.7
  249.9 22.2 reduce-scatter.3
  279.8 20.0 reduce-scatter.5
  307.5 19.1 reduce-scatter.7
where the time goes:
time: 349 us; the launch traced here: 348 us
  waiting for transfers between devices  240 us (69%)
  blocking collectives  30.7 us (9%)
  starting transfers between devices  27.6 us (8%)
  matrix products  25.9 us (7%)
  between operations  14.5 us (4%)
  local copies, waits for them, and re-layouts  6.3 us (2%)
    ppermute x8, waiting for transfers between devices, passed_along(): return lax.ppermute(shard, axis, pairs)  117 us
    reduce_scatter x3, waiting for transfers between devices, local(): lax.psum_scatter(partial_value, 'col', scatter_dimension=1, tiled=True)  61.8 us
    all_gather x2, waiting for transfers between devices, advance(): return matmul(lax.all_gather(state, 'col', axis=1, tiled=True), matrix)  38.7 us
    dot_general x17, matrix products, matmul(): jnp.dot(left, right, precision=lax.Precision.HIGHEST, preferred_element_t...  25.4 us
    ppermute x8, starting transfers between devices, passed_along(): return lax.ppermute(shard, axis, pairs)  24 us
    all_gather x1, waiting for transfers between devices, local(): whole = lax.all_gather(element, 'col', axis=1, tiled=True)  18.5 us
    all_gather x3, blocking collectives, smooth_step(): residual_full = lax.all_gather(residual, 'col', axis=1, tiled=True)  17.5 us
    all_gather x1, blocking collectives, local(): filtered_full = lax.all_gather(filtered, 'col', axis=2, tiled=True)  7.28 us
  transfers between devices with their start and end apart: 15, of which 15 were waited for; matrix products, arithmetic and copies ran while one was open for 3% of the time, Pallas kernels for 0%

commit v1 on v0

--- a/solution.py
+++ b/solution.py
@@ -49,7 +49,15 @@
     trans_cols = (
         coupling.astype(jnp.float32) * mask_cols[None] + diag_cols[None] * persist[:, None, :]
     )
-    rows_coupling = lax.all_to_all(coupling, "col", split_axis=1, concat_axis=2, tiled=True)
+    rows_coupling = jnp.concatenate(
+        lax.all_to_all(
+            jnp.stack(jnp.split(coupling, lax.axis_size("col"), axis=1)),
+            split_axis=0,
+            axis_name="col",
+            concat_axis=0,
+        ),
+        axis=2,
+    )
     trans_rows = (
         rows_coupling.astype(jnp.float32) * mask_rows[None] + diag_rows[None] * persist[:, :, None]
     )

time: 349 us -> 349 us (level)
  no operation moved by 1% of the time
where the time goes in v1:
time: 349 us; the launch traced here: 348 us
  waiting for transfers between devices  239 us (68%)
  blocking collectives  30.7 us (9%)
  starting transfers between devices  27.6 us (8%)
  matrix products  26.4 us (8%)
  between operations  14.5 us (4%)
  local copies, waits for them, and re-layouts  6.08 us (2%)
    ppermute x8, waiting for transfers between devices, passed_along(): return lax.ppermute(shard, axis, pairs)  117 us
    reduce_scatter x3, waiting for transfers between devices, local(): lax.psum_scatter(partial_value, 'col', scatter_dimension=1, tiled=True)  61.8 us
    all_gather x2, waiting for transfers between devices, advance(): return matmul(lax.all_gather(state, 'col', axis=1, tiled=True), matrix)  38.7 us
    dot_general x17, matrix products, matmul(): jnp.dot(left, right, precision=lax.Precision.HIGHEST, preferred_element_t...  26 us
    ppermute x8, starting transfers between devices, passed_along(): return lax.ppermute(shard, axis, pairs)  24 us
    all_gather x1, waiting for transfers between devices, local(): whole = lax.all_gather(element, 'col', axis=1, tiled=True)  18.5 us
    all_gather x3, blocking collectives, smooth_step(): residual_full = lax.all_gather(residual, 'col', axis=1, tiled=True)  17.5 us
    all_gather x1, blocking collectives, local(): filtered_full = lax.all_gather(filtered, 'col', axis=2, tiled=True)  7.28 us
  transfers between devices with their start and end apart: 15, of which 15 were waited for; matrix products, arithmetic and copies ran while one was open for 3% of the time, Pallas kernels for 0%

profile of v1, /device:TPU:0, one launch (start us, length us, event | category | flops | bytes accessed | tf_op | source)
XLA Modules:
  0.0 347.8 jit_solution(642039474976971426)
XLA Ops:
  10.4 20.2 %all-gather.4.cloned.1.call-done = f32[640,512]{1,0:T(8,128)} async-done(((f32[640,128]{1,0:T(8,128)}), f32[640,512]{1,0:T(8,128)}) %all-gather.4.cloned.1.call-update) | async-done | bytes 1310736 | tf_op jit(solution)/shard_map/all_gather | solution.py:18
  33.9 18.4 %all-gather.6.cloned.1.call-done = f32[640,512]{1,0:T(8,128)} async-done(((f32[640,128]{1,0:T(8,128)}), f32[640,512]{1,0:T(8,128)}) %all-gather.6.cloned.1.call-update) | async-done | bytes 1310736 | tf_op jit(solution)/shard_map/all_gather | solution.py:18
  55.6 18.5 %all-gather.8.cloned.1.call-done = f32[640,512]{1,0:T(8,128)} async-done(((f32[640,128]{1,0:T(8,128)}), f32[640,512]{1,0:T(8,128)}) %all-gather.8.cloned.1.call-update) | async-done | bytes 1310736 | tf_op jit(solution)/shard_map/all_gather | solution.py:77
  74.1 3.4 collective-permute-start
  78.5 27.7 %collective-permute-done = f32[640,512]{1,0:T(8,128)S(1)} collective-permute-done((f32[640,512]{1,0:T(8,128)}, f32[640,512]{1,0:T(8,128)S(1)}, u32[]{:S(2)}, u32[]{:S(2)}) %collective-permute-start) | collective-permute-done | bytes 1310752 | tf_op jit(solution)/shard_map/ppermute | solution.py:10
  106.2 3.9 %fusion = f32[640,512]{1,0:T(8,128)S(1)} fusion(f32[640,512]{1,0:T(8,128)} %all-gather.8.cloned.1.call-done, f32[640,512]{1,0:T(8,128)S(1)} %collective-permute-done, f32[128,512]{1,0:T(8,128)S(1)} %slice.85, pred[]{:T(512)S(6)} %ge.11), kind=kOutput, calls=%fused_computation.2 | convolution fusion | flops 2013921280 | bytes 5242881 | tf_op jit(solution)/shard_map/dot_general | solution.py:14
  110.1 6.3 %collective-permute-start.1 = (f32[640,512]{1,0:T(8,128)S(1)}, f32[640,512]{1,0:T(8,128)}, u32[]{:S(2)}, u32[]{:S(2)}) collective-permute-start(f32[640,512]{1,0:T(8,128)S(1)} %fusion), channel_id=1, source_target_pairs={{0,8},{4,12},{8,16},{12,20},{16,24},{20,28},{1,9},{5,13},{9,17},{1... | collective-permute-start | bytes 3932168 | tf_op jit(solution)/shard_map/ppermute | solution.py:10
  116.4 26.5 %collective-permute-done.1 = f32[640,512]{1,0:T(8,128)} collective-permute-done((f32[640,512]{1,0:T(8,128)S(1)}, f32[640,512]{1,0:T(8,128)}, u32[]{:S(2)}, u32[]{:S(2)}) %collective-permute-start.1) | collective-permute-done | bytes 1310752 | tf_op jit(solution)/shard_map/ppermute | solution.py:10
  142.8 3.6 %fusion.1 = f32[640,512]{1,0:T(8,128)S(1)} fusion(f32[640,512]{1,0:T(8,128)S(1)} %fusion, f32[640,512]{1,0:T(8,128)} %collective-permute-done.1, f32[128,512]{1,0:T(8,128)S(1)} %slice.87, pred[]{:T(512)S(6)} %ge.10), kind=kOutput, calls=%fused_computation.3 | convolution fusion | flops 2013921280 | bytes 5242881 | tf_op jit(solution)/shard_map/dot_general | solution.py:14
  146.4 6.5 %collective-permute-start.2 = (f32[640,512]{1,0:T(8,128)S(1)}, f32[640,512]{1,0:T(8,128)}, u32[]{:S(2)}, u32[]{:S(2)}) collective-permute-start(f32[640,512]{1,0:T(8,128)S(1)} %fusion.1), channel_id=1, source_target_pairs={{0,16},{4,20},{8,24},{12,28},{1,17},{5,21},{9,25},{13,29},{2,18},{... | collective-permute-start | bytes 3932168 | tf_op jit(solution)/shard_map/ppermute | solution.py:10
  166.0 12.6 %collective-permute-done.2 = f32[640,512]{1,0:T(8,128)} collective-permute-done((f32[640,512]{1,0:T(8,128)S(1)}, f32[640,512]{1,0:T(8,128)}, u32[]{:S(2)}, u32[]{:S(2)}) %collective-permute-start.2) | collective-permute-done | bytes 1310752 | tf_op jit(solution)/shard_map/ppermute | solution.py:10
  178.6 3.5 %fusion.39 = f32[640,512]{1,0:T(8,128)S(1)} fusion(f32[640,512]{1,0:T(8,128)} %collective-permute-done.2, f32[640,512]{1,0:T(8,128)S(1)} %fusion.1), kind=kOutput, calls=%fused_computation.81 | convolution fusion | flops 2013265920 | bytes 3670016 | tf_op jit(solution)/shard_map/dot_general | solution.py:14
  186.7 5.9 %all_gather.27 = f32[128,512]{1,0:T(8,128)S(1)} all-gather(f32[128,128]{1,0:T(8,128)S(1)} %collective-permute-done.3), channel_id=1, replica_groups=mesh['tm'=8,'col'=4] {'col'}, dimensions={1}, use_global_device_ids=true | all-gather | bytes 327680 | tf_op jit(solution)/shard_map/all_gather | solution.py:90
  193.1 7.3 %all_gather.28 = f32[2,128,512]{2,1,0:T(8,128)S(1)} all-gather(f32[2,128,128]{2,1,0:T(8,128)S(1)} %fusion.2), channel_id=1, replica_groups=mesh['tm'=8,'col'=4] {'col'}, dimensions={2}, use_global_device_ids=true | all-gather | bytes 655360 | tf_op jit(solution)/shard_map/all_gather | solution.py:100
  200.8 5.9 %all_gather.29 = f32[128,512]{1,0:T(8,128)S(1)} all-gather(f32[128,128]{1,0:T(8,128)S(1)} %get-tuple-element.10), channel_id=1, replica_groups=mesh['tm'=8,'col'=4] {'col'}, dimensions={1}, use_global_device_ids=true | all-gather | bytes 327680 | tf_op jit(solution)/shard_map/all_gather | solution.py:24
  207.4 5.9 %all_gather.30 = f32[128,512]{1,0:T(8,128)S(1)} all-gather(f32[128,128]{1,0:T(8,128)S(1)} %convolution_subtract_fusion), channel_id=1, replica_groups=mesh['tm'=8,'col'=4] {'col'}, dimensions={1}, use_global_device_ids=true | all-gather | bytes 327680 | tf_op jit(solution)/shard_map/all_gather | solution.py:24
  216.3 32.3 %collective-permute-done.4 = f32[128,128]{1,0:T(8,128)S(1)} collective-permute-done((f32[128,128]{1,0:T(8,128)S(1)}, f32[128,128]{1,0:T(8,128)S(1)}, u32[]{:S(2)}, u32[]{:S(2)}) %collective-permute-start.4) | collective-permute-done | bytes 65568 | tf_op jit(solution)/shard_map/ppermute | solution.py:10
  249.8 22.4 %reduce-scatter.4.cloned.1.call-done = f32[128,128]{1,0:T(8,128)} async-done(((f32[128,512]{1,0:T(8,128)}), f32[128,128]{1,0:T(8,128)}) %reduce-scatter.4.cloned.1.call-update) | async-done | bytes 65552 | tf_op jit(solution)/shard_map/reduce_scatter | solution.py:121
  273.5 5.0 %collective-permute-done.5 = f32[128,128]{1,0:T(8,128)S(1)} collective-permute-done((f32[128,128]{1,0:T(8,128)}, f32[128,128]{1,0:T(8,128)S(1)}, u32[]{:S(2)}, u32[]{:S(2)}) %collective-permute-start.5) | collective-permute-done | bytes 65568 | tf_op jit(solution)/shard_map/ppermute | solution.py:10
  279.7 20.2 %reduce-scatter.6.cloned.1.call-done = f32[128,128]{1,0:T(8,128)} async-done(((f32[128,512]{1,0:T(8,128)}), f32[128,128]{1,0:T(8,128)}) %reduce-scatter.6.cloned.1.call-update) | async-done | bytes 65552 | tf_op jit(solution)/shard_map/reduce_scatter | solution.py:121
  301.2 5.0 %collective-permute-done.6 = f32[128,128]{1,0:T(8,128)S(1)} collective-permute-done((f32[128,128]{1,0:T(8,128)}, f32[128,128]{1,0:T(8,128)S(1)}, u32[]{:S(2)}, u32[]{:S(2)}) %collective-permute-start.6) | collective-permute-done | bytes 65568 | tf_op jit(solution)/shard_map/ppermute | solution.py:10
  307.3 19.3 %reduce-scatter.8.cloned.1.call-done = f32[128,128]{1,0:T(8,128)} async-done(((f32[128,512]{1,0:T(8,128)}), f32[128,128]{1,0:T(8,128)}) %reduce-scatter.8.cloned.1.call-update) | async-done | bytes 65552 | tf_op jit(solution)/shard_map/reduce_scatter | solution.py:121
  327.9 6.3 %collective-permute-done.7 = f32[128,128]{1,0:T(8,128)S(1)} collective-permute-done((f32[128,128]{1,0:T(8,128)}, f32[128,128]{1,0:T(8,128)S(1)}, u32[]{:S(2)}, u32[]{:S(2)}) %collective-permute-start.7) | collective-permute-done | bytes 65568 | tf_op jit(solution)/shard_map/ppermute | solution.py:10
  334.1 5.8 %all_gather.31 = f32[128,512]{1,0:T(8,128)S(1)} all-gather(f32[128,128]{1,0:T(8,128)S(1)} %get-tuple-element.6), channel_id=1, replica_groups=mesh['tm'=8,'col'=4] {'col'}, dimensions={1}, use_global_device_ids=true | all-gather | bytes 327680 | tf_op jit(solution)/shard_map/all_gather | solution.py:24
  (84 shorter events, 41.1 us)
Async XLA Ops:
  7.2 3.1 copy-start.9
  7.2 3.1 copy-start.5
  7.2 23.4 %all-gather.4.cloned.1.call-start = ((), (), s32[]{:S(2)}) async-start(), calls=%async_computation.4 | async-start | bytes 1638400 | tf_op jit(solution)/shard_map/all_gather | solution.py:18
  8.1 44.3 %all-gather.6.cloned.1.call-start = ((), (), s32[]{:S(2)}) async-start(), calls=%async_computation.5 | async-start | bytes 1638400 | tf_op jit(solution)/shard_map/all_gather | solution.py:18
  33.9 40.2 %all-gather.8.cloned.1.call-start = ((), (), s32[]{:S(2)}) async-start(), calls=%async_computation.6 | async-start | bytes 1638400 | tf_op jit(solution)/shard_map/all_gather | solution.py:77
  74.1 32.1 %collective-permute-start = (f32[640,512]{1,0:T(8,128)}, f32[640,512]{1,0:T(8,128)S(1)}, u32[]{:S(2)}, u32[]{:S(2)}) collective-permute-start(f32[640,512]{1,0:T(8,128)} %all-gather.8.cloned.1.call-done), channel_id=1, source_target_pairs={{0,4},{4,8},{8,12},{12,16},{16,20},{20,24},{24,28},{1,5},{5,9},{9,... | collective-permute-start | bytes 3932168 | tf_op jit(solution)/shard_map/ppermute | solution.py:10
  110.1 32.8 %collective-permute-start.1 = (f32[640,512]{1,0:T(8,128)S(1)}, f32[640,512]{1,0:T(8,128)}, u32[]{:S(2)}, u32[]{:S(2)}) collective-permute-start(f32[640,512]{1,0:T(8,128)S(1)} %fusion), channel_id=1, source_target_pairs={{0,8},{4,12},{8,16},{12,20},{16,24},{20,28},{1,9},{5,13},{9,17},{1... | collective-permute-start | bytes 3932168 | tf_op jit(solution)/shard_map/ppermute | solution.py:10
  146.4 32.2 %collective-permute-start.2 = (f32[640,512]{1,0:T(8,128)S(1)}, f32[640,512]{1,0:T(8,128)}, u32[]{:S(2)}, u32[]{:S(2)}) collective-permute-start(f32[640,512]{1,0:T(8,128)S(1)} %fusion.1), channel_id=1, source_target_pairs={{0,16},{4,20},{8,24},{12,28},{1,17},{5,21},{9,25},{13,29},{2,18},{... | collective-permute-start | bytes 3932168 | tf_op jit(solution)/shard_map/ppermute | solution.py:10
  156.5 9.4 %all-to-all-start = ((bf16[4,2,128,128]{2,3,1,0:T(8,128)(2,1)}), bf16[4,2,128,128]{2,3,1,0:T(8,128)(2,1)S(1)}, u32[]{:S(2)}, u32[]{:S(2)}) async-start(bf16[4,2,128,128]{2,3,1,0:T(8,128)(2,1)} %pad_maximum_fusion), calls=%async_computation | async-start | bytes 524288 | tf_op jit(solution)/shard_map/all_to_all | solution.py:53
  159.9 112.2 %reduce-scatter.4.cloned.1.call-start = ((), (), s32[]{:S(2)}) async-start(), calls=%async_computation.7 | async-start | bytes 327680 | tf_op jit(solution)/shard_map/reduce_scatter | solution.py:121
  165.9 18.9 %copy-start.6 = (f32[128,512]{0,1:T(8,128)S(1)}, f32[128,512]{0,1:T(8,128)}, u32[]{:S(2)}) copy-start(f32[128,512]{0,1:T(8,128)} %fusion.15) | copy-start | bytes 786436
  166.0 18.9 %copy-start.7 = (f32[128,512]{0,1:T(8,128)S(1)}, f32[128,512]{0,1:T(8,128)}, u32[]{:S(2)}) copy-start(f32[128,512]{0,1:T(8,128)} %fusion.18) | copy-start | bytes 786436
  182.2 10.5 %copy-start = (f32[640,128]{1,0:T(8,128)S(1)}, f32[640,128]{1,0:T(8,128)}, u32[]{:S(2)}) copy-start(f32[640,128]{1,0:T(8,128)} %convolution_add_fusion.3) | copy-start | bytes 983044
  182.2 10.5 %copy-start.1 = (f32[640,128]{1,0:T(8,128)S(1)}, f32[640,128]{1,0:T(8,128)}, u32[]{:S(2)}) copy-start(f32[640,128]{1,0:T(8,128)} %convolution_add_fusion.2) | copy-start | bytes 983044
  182.2 4.5 %collective-permute-start.3 = (f32[128,128]{1,0:T(8,128)S(1)}, f32[128,128]{1,0:T(8,128)S(1)}, u32[]{:S(2)}, u32[]{:S(2)}) collective-permute-start(f32[128,128]{1,0:T(8,128)S(1)} %fusion.22), channel_id=1, source_target_pairs={{0,4},{4,8},{8,12},{12,16},{16,20},{20,24},{24,28},{1,5},{5,9},{9,... | collective-permute-start | bytes 196616 | tf_op jit(solution)/shard_map/ppermute | solution.py:10
  184.9 28.4 %copy-start.2 = (f32[2,128,512]{1,2,0:T(8,128)}, f32[2,128,512]{1,2,0:T(8,128)S(1)}, u32[]{:S(2)}) copy-start(f32[2,128,512]{1,2,0:T(8,128)S(1)} %fusion.6) | copy-start | bytes 1572868
  193.1 146.8 %copy-start.4 = (f32[2,128,128]{2,1,0:T(8,128)}, f32[2,128,128]{2,1,0:T(8,128)S(1)}, u32[]{:S(2)}) copy-start(f32[2,128,128]{2,1,0:T(8,128)S(1)} %fusion.2) | copy-start | bytes 393220
  213.7 34.9 %collective-permute-start.4 = (f32[128,128]{1,0:T(8,128)S(1)}, f32[128,128]{1,0:T(8,128)S(1)}, u32[]{:S(2)}, u32[]{:S(2)}) collective-permute-start(f32[128,128]{1,0:T(8,128)S(1)} %convolution_add_fusion.5), channel_id=1, source_target_pairs={{4,0},{8,4},{12,8},{16,12},{20,16},{24,20},{28,24},{5,1},{9,5},{13... | collective-permute-start | bytes 196616 | tf_op jit(solution)/shard_map/ppermute | solution.py:10
  249.7 50.1 %reduce-scatter.6.cloned.1.call-start = ((), (), s32[]{:S(2)}) async-start(), calls=%async_computation.8 | async-start | bytes 327680 | tf_op jit(solution)/shard_map/reduce_scatter | solution.py:121
  272.1 6.4 %collective-permute-start.5 = (f32[128,128]{1,0:T(8,128)}, f32[128,128]{1,0:T(8,128)S(1)}, u32[]{:S(2)}, u32[]{:S(2)}) collective-permute-start(f32[128,128]{1,0:T(8,128)} %reduce-scatter.4.cloned.1.call-done), channel_id=1, source_target_pairs={{4,0},{8,4},{12,8},{16,12},{20,16},{24,20},{28,24},{5,1},{9,5},{13... | collective-permute-start | bytes 196616 | tf_op jit(solution)/shard_map/ppermute | solution.py:10
  279.6 47.0 %reduce-scatter.8.cloned.1.call-start = ((), (), s32[]{:S(2)}) async-start(), calls=%async_computation.9 | async-start | bytes 327680 | tf_op jit(solution)/shard_map/reduce_scatter | solution.py:121
  299.8 6.4 %collective-permute-start.6 = (f32[128,128]{1,0:T(8,128)}, f32[128,128]{1,0:T(8,128)S(1)}, u32[]{:S(2)}, u32[]{:S(2)}) collective-permute-start(f32[128,128]{1,0:T(8,128)} %reduce-scatter.6.cloned.1.call-done), channel_id=1, source_target_pairs={{8,0},{12,4},{16,8},{20,12},{24,16},{28,20},{9,1},{13,5},{17,9},{2... | collective-permute-start | bytes 196616 | tf_op jit(solution)/shard_map/ppermute | solution.py:10
  301.2 38.7 %copy-start.3 = (f32[2,128,512]{1,2,0:T(8,128)S(1)}, f32[2,128,512]{1,2,0:T(8,128)}, u32[]{:S(2)}) copy-start(f32[2,128,512]{1,2,0:T(8,128)} %copy-done.2) | copy-start | bytes 1572868
  326.6 7.5 %collective-permute-start.7 = (f32[128,128]{1,0:T(8,128)}, f32[128,128]{1,0:T(8,128)S(1)}, u32[]{:S(2)}, u32[]{:S(2)}) collective-permute-start(f32[128,128]{1,0:T(8,128)} %reduce-scatter.8.cloned.1.call-done), channel_id=1, source_target_pairs={{16,0},{20,4},{24,8},{28,12},{17,1},{21,5},{25,9},{29,13},{18,2},{... | collective-permute-start | bytes 196616 | tf_op jit(solution)/shard_map/ppermute | solution.py:10
  (1 other events, 2.0 us)
Sparse Core Ops, SparseCore 0:
  9.6 21.0 all-gather.3
  34.0 18.3 all-gather.5
  55.7 18.3 all-gather.7
  249.8 22.2 reduce-scatter.3
  279.7 20.0 reduce-scatter.5
  307.4 19.1 reduce-scatter.7
